TPU v7x, 32 devices: a whole 2x2x4 slice. The times are simulated.
32 devices in a mesh: dp: 8 (over y, x, core), tensor: 4 (over z).
Axes of the slice: x: 2, y: 2, z: 4, core: 2. Of those that a mesh axis runs over, the one named last changes fastest.
Arguments:
- inputs: bfloat16 [4096, 2048], P('dp'), may hold values from -6 to 6
- active: int32 [4096], P('dp'), may hold values from 0 to 1, as said below
- block_table: int32 [16], replicated, may hold values from 0 to 15, as said below
- gain_one: bfloat16 [2048], replicated, may hold values from 0.099609375 to 1.8984375
- w_query: bfloat16 [2048, 2048], P(None, 'tensor'), may hold values from -0.125 to 0.125
- w_key: bfloat16 [2048, 1024], P(None, 'tensor'), may hold values from -0.125 to 0.125
- w_value: bfloat16 [2048, 1024], P(None, 'tensor'), may hold values from -0.125 to 0.125
- w_out: bfloat16 [2048, 2048], P('tensor'), may hold values from -4 to 4
- gain_two: bfloat16 [2048], replicated, may hold values from 0.099609375 to 1.8984375
- w_gate: bfloat16 [2048, 5632], P(None, 'tensor'), may hold values from -0.125 to 0.125
- w_up: bfloat16 [2048, 5632], P(None, 'tensor'), may hold values from -0.125 to 0.125
- w_down: bfloat16 [5632, 2048], P('tensor'), may hold values from -0.078125 to 0.078125
- cotangent: bfloat16 [4096, 2048], P('dp'), may hold values from -6 to 6
Outputs:
- output: bfloat16 [4096, 2048], P('dp')
- grad_input: float32 [4096, 2048], P('dp')
- grad_gain_one: float32 [2048], replicated
- grad_w_query: float32 [2048, 2048], P(None, 'tensor')
- grad_w_key: float32 [2048, 1024], P(None, 'tensor')
- grad_w_value: float32 [2048, 1024], P(None, 'tensor')
- grad_w_out: float32 [2048, 2048], P('tensor')
- grad_gain_two: float32 [2048], replicated
- grad_w_gate: float32 [2048, 5632], P(None, 'tensor')
- grad_w_up: float32 [2048, 5632], P(None, 'tensor')
- grad_w_down: float32 [5632, 2048], P('tensor')
Inputs may be any that keep to these rules, and one draw needn't show every extreme that they name: `active`: 0 or 1 for every token; the share of 1s differs from one causal block to another. `block_table`: each causal block appears once; entries 2i and 2i+1 sum to 15.
All inputs are finite; a program needn't handle non-finite values.
Results may differ from a plain program's by a relative error of at most 0.014.
Values may be sent and summed in bfloat16 or wider, within the bound.
No kernel may reach another device: no remote copies, remote signals or barrier semaphores. Data moves between devices by JAX's collectives and lax.ppermute only.
A program may use at most 256 MiB of HBM per device.

v0:
```python
import jax
import jax.numpy as jnp
from jax import lax
from jax.sharding import PartitionSpec as P

HEAD_DIM = 128
EPS = 1e-05
MASKED_SCORE = -1e30


def rms_norm(values, scales):
    return values * lax.rsqrt(jnp.mean(values * values, axis=-1, keepdims=True) + EPS) * scales


def rotate(values, cos_table, sin_table):
    middle = values.shape[-1] // 2
    leading = values[..., :middle]
    trailing = values[..., middle:]
    return jnp.concatenate(
        [leading * cos_table - trailing * sin_table, trailing * cos_table + leading * sin_table],
        axis=-1,
    )


def angles_of(positions, head_size):
    frequency = 10000.0 ** (-jnp.arange(0, head_size, 2, dtype=jnp.float32) / head_size)
    angles = positions.astype(jnp.float32)[:, None] * frequency[None, :]
    return (jnp.cos(angles)[:, None, :], jnp.sin(angles)[:, None, :])


def swiglu(gate_value, up_value):
    return jax.nn.silu(gate_value) * up_value


def left_trans(left, right):
    return lax.dot_general(
        left, right, (((0,), (0,)), ((), ())), preferred_element_type=jnp.float32
    )


def right_trans(left, right):
    return lax.dot_general(
        left, right, (((1,), (1,)), ((), ())), preferred_element_type=jnp.float32
    )


def partner_perm(axis_size, mask):
    return [(index, index ^ mask) for index in range(axis_size)]


def permute_sum(parts, dims, axis):
    size = lax.axis_size(axis)
    steps = size.bit_length() - 1
    assert 1 << steps == size
    me = lax.axis_index(axis)
    pieces = list(parts)
    for step in range(steps):
        bit = me >> step & 1
        keep, send = ([], [])
        for piece, dim in zip(pieces, dims):
            half = piece.shape[dim] // 2
            keep.append(lax.dynamic_slice_in_dim(piece, bit * half, half, axis=dim))
            send.append(
                lax.dynamic_slice_in_dim(piece, (1 - bit) * half, half, axis=dim).astype(
                    jnp.bfloat16
                )
            )
        got = lax.ppermute(send, axis, partner_perm(size, 1 << step))
        pieces = [mine + theirs.astype(jnp.float32) for mine, theirs in zip(keep, got)]
    pieces = [piece.astype(jnp.bfloat16) for piece in pieces]
    for step in reversed(range(steps)):
        first = me >> step & 1 == 0
        got = lax.ppermute(pieces, axis, partner_perm(size, 1 << step))
        pieces = [
            jnp.concatenate(
                [jnp.where(first, mine, theirs), jnp.where(first, theirs, mine)], axis=dim
            )
            for mine, theirs, dim in zip(pieces, got, dims)
        ]
    return [piece.astype(jnp.float32) for piece in pieces]


def permute_allsum(value, axis):
    size = lax.axis_size(axis)
    steps = size.bit_length() - 1
    for step in range(steps):
        value = value + lax.ppermute(value, axis, partner_perm(size, 1 << step))
    return value


def on_device(
    inputs,
    active,
    block_table,
    gain_one,
    w_query,
    w_key,
    w_value,
    w_out,
    gain_two,
    w_gate,
    w_up,
    w_down,
    cotangent,
):
    row_count = inputs.shape[0]
    local_heads = w_query.shape[1] // HEAD_DIM
    local_groups = w_key.shape[1] // HEAD_DIM
    group_size = local_heads // local_groups
    half_rows = row_count // 2
    length = row_count * lax.axis_size("dp")
    score_scale = HEAD_DIM ** (-0.5)
    key_pos = (
        block_table[:, None] * half_rows + jnp.arange(half_rows, dtype=jnp.int32)[None, :]
    ).reshape(length)
    row_start = lax.axis_index("dp") * row_count
    query_pos = lax.dynamic_slice_in_dim(key_pos, row_start, row_count)
    slot_ids = jnp.arange(length, dtype=jnp.int32)
    own_ids = row_start + jnp.arange(row_count, dtype=jnp.int32)
    cos_table, sin_table = angles_of(query_pos, HEAD_DIM)
    keep_rows = active.astype(jnp.float32)[:, None]
    source = inputs.astype(jnp.float32)
    normed_full, norm_one_back = jax.vjp(rms_norm, source, gain_one.astype(jnp.float32))
    normed = normed_full.astype(jnp.bfloat16)
    query_raw = jnp.dot(normed, w_query, preferred_element_type=jnp.float32).reshape(
        row_count, local_heads, HEAD_DIM
    )
    key_raw = jnp.dot(normed, w_key, preferred_element_type=jnp.float32).reshape(
        row_count, local_groups, HEAD_DIM
    )
    value_low = jnp.dot(normed, w_value, preferred_element_type=jnp.float32).astype(jnp.bfloat16)
    query_low = (
        rotate(query_raw, cos_table, sin_table)
        .reshape(row_count, local_heads * HEAD_DIM)
        .astype(jnp.bfloat16)
    )
    key_low = (
        rotate(key_raw, cos_table, sin_table)
        .reshape(row_count, local_groups * HEAD_DIM)
        .astype(jnp.bfloat16)
    )
    alive_low = active.astype(jnp.bfloat16)

    def allowed_of(alive_all):
        return (key_pos[None, :] <= query_pos[:, None]) & (
            (alive_all[None, :] > 0) | (slot_ids[None, :] == own_ids[:, None])
        )

    def head_scores(head_index, keys_all, allowed):
        query_part = query_low[:, head_index * HEAD_DIM : (head_index + 1) * HEAD_DIM]
        group_index = head_index // group_size
        key_part = keys_all[:, group_index * HEAD_DIM : (group_index + 1) * HEAD_DIM]
        raw_scores = right_trans(query_part, key_part) * score_scale
        return jnp.where(allowed, raw_scores, MASKED_SCORE)

    kv_width = local_groups * HEAD_DIM
    all_kv = lax.all_gather(jnp.concatenate([key_low, value_low], axis=1), "dp", axis=0, tiled=True)
    all_keys = all_kv[:, :kv_width]
    all_values = all_kv[:, kv_width:]
    all_alive = lax.all_gather(alive_low, "dp", axis=0, tiled=True)
    allowed_fwd = allowed_of(all_alive)
    mixed_parts = []
    lse_parts = []
    for head_index in range(local_heads):
        masked = head_scores(head_index, all_keys, allowed_fwd)
        row_max = jnp.max(masked, axis=1, keepdims=True)
        shifted = jnp.exp(masked - row_max)
        row_total = jnp.sum(shifted, axis=1, keepdims=True)
        probs_low = (shifted / row_total).astype(jnp.bfloat16)
        lse_parts.append(row_max + jnp.log(row_total))
        group_index = head_index // group_size
        value_part = all_values[:, group_index * HEAD_DIM : (group_index + 1) * HEAD_DIM]
        mixed_parts.append(jnp.dot(probs_low, value_part, preferred_element_type=jnp.float32))
    attended = jnp.concatenate(mixed_parts, axis=1).astype(jnp.bfloat16)
    branch = lax.psum(
        jnp.dot(attended, w_out, preferred_element_type=jnp.float32).astype(jnp.bfloat16), "tensor"
    ).astype(jnp.float32)
    middle = source + keep_rows * branch
    normed_two_full, norm_two_back = jax.vjp(rms_norm, middle, gain_two.astype(jnp.float32))
    normed_two = normed_two_full.astype(jnp.bfloat16)
    gate_value = jnp.dot(normed_two, w_gate, preferred_element_type=jnp.float32)
    up_value = jnp.dot(normed_two, w_up, preferred_element_type=jnp.float32)
    hidden_full, swiglu_back = jax.vjp(swiglu, gate_value, up_value)
    hidden = hidden_full.astype(jnp.bfloat16)
    down_sum = lax.psum(
        jnp.dot(hidden, w_down, preferred_element_type=jnp.float32).astype(jnp.bfloat16), "tensor"
    ).astype(jnp.float32)
    output = (middle + keep_rows * down_sum).astype(jnp.bfloat16)
    grad_out = cotangent.astype(jnp.float32)
    d_down = (keep_rows * grad_out).astype(jnp.bfloat16)
    grad_w_down = left_trans(hidden, d_down)
    d_hidden = right_trans(d_down, w_down)
    d_gate_full, d_up_full = swiglu_back(d_hidden)
    d_gate = d_gate_full.astype(jnp.bfloat16)
    d_up = d_up_full.astype(jnp.bfloat16)
    grad_w_gate = left_trans(normed_two, d_gate)
    grad_w_up = left_trans(normed_two, d_up)
    d_normed_two = lax.psum(
        (right_trans(d_gate, w_gate) + right_trans(d_up, w_up)).astype(jnp.bfloat16), "tensor"
    ).astype(jnp.float32)
    d_middle_norm, grad_gain_two = norm_two_back(d_normed_two)
    grad_middle = grad_out + d_middle_norm
    d_branch = (keep_rows * grad_middle).astype(jnp.bfloat16)
    grad_w_out = left_trans(attended, d_branch)
    d_attended = right_trans(d_branch, w_out).astype(jnp.bfloat16)
    back_keys, back_values = (all_keys, all_values)
    allowed_back = allowed_fwd
    d_query_parts = []
    d_key_parts = [
        jnp.zeros((length, HEAD_DIM), jnp.float32) for group_index in range(local_groups)
    ]
    d_value_parts = [
        jnp.zeros((length, HEAD_DIM), jnp.float32) for group_index in range(local_groups)
    ]
    for head_index in range(local_heads):
        group_index = head_index // group_size
        masked = head_scores(head_index, back_keys, allowed_back)
        probs = jnp.where(allowed_back, jnp.exp(masked - lse_parts[head_index]), 0.0)
        probs_low = probs.astype(jnp.bfloat16)
        d_out_part = d_attended[:, head_index * HEAD_DIM : (head_index + 1) * HEAD_DIM]
        key_part = back_keys[:, group_index * HEAD_DIM : (group_index + 1) * HEAD_DIM]
        value_part = back_values[:, group_index * HEAD_DIM : (group_index + 1) * HEAD_DIM]
        query_part = query_low[:, head_index * HEAD_DIM : (head_index + 1) * HEAD_DIM]
        d_probs = right_trans(d_out_part, value_part)
        row_delta = jnp.sum(probs * d_probs, axis=1, keepdims=True)
        d_scores = (probs * (d_probs - row_delta)).astype(jnp.bfloat16)
        d_query_parts.append(
            jnp.dot(d_scores, key_part, preferred_element_type=jnp.float32) * score_scale
        )
        d_key_parts[group_index] = (
            d_key_parts[group_index] + left_trans(d_scores, query_part) * score_scale
        )
        d_value_parts[group_index] = d_value_parts[group_index] + left_trans(probs_low, d_out_part)
    d_key_all = jnp.concatenate(d_key_parts, axis=1)
    d_value_all = jnp.concatenate(d_value_parts, axis=1)
    d_kv_own = lax.psum_scatter(
        jnp.concatenate([d_key_all, d_value_all], axis=1).astype(jnp.bfloat16),
        "dp",
        scatter_dimension=0,
        tiled=True,
    ).astype(jnp.float32)
    d_key_own = d_kv_own[:, :kv_width]
    d_value_own = d_kv_own[:, kv_width:]
    d_queries = jnp.concatenate(d_query_parts, axis=1).reshape(row_count, local_heads, HEAD_DIM)
    d_query_low = (
        rotate(d_queries, cos_table, -sin_table)
        .reshape(row_count, local_heads * HEAD_DIM)
        .astype(jnp.bfloat16)
    )
    d_key_low = (
        rotate(d_key_own.reshape(row_count, local_groups, HEAD_DIM), cos_table, -sin_table)
        .reshape(row_count, local_groups * HEAD_DIM)
        .astype(jnp.bfloat16)
    )
    d_value_low = d_value_own.astype(jnp.bfloat16)
    grad_w_query = left_trans(normed, d_query_low)
    grad_w_key = left_trans(normed, d_key_low)
    grad_w_value = left_trans(normed, d_value_low)
    d_normed_part = (
        right_trans(d_query_low, w_query)
        + right_trans(d_key_low, w_key)
        + right_trans(d_value_low, w_value)
    )
    d_normed = lax.psum(d_normed_part.astype(jnp.bfloat16), "tensor").astype(jnp.float32)
    d_source_norm, grad_gain_one = norm_one_back(d_normed)
    grad_input = grad_middle + d_source_norm
    grad_gain_one = permute_allsum(grad_gain_one, "dp")
    grad_gain_two = permute_allsum(grad_gain_two, "dp")
    grad_w_gate, grad_w_up, grad_w_down = permute_sum(
        [grad_w_gate, grad_w_up, grad_w_down], [0, 0, 1], "dp"
    )
    (grad_w_out,) = permute_sum([grad_w_out], [1], "dp")
    grad_w_query, grad_w_key, grad_w_value = permute_sum(
        [grad_w_query, grad_w_key, grad_w_value], [0, 0, 0], "dp"
    )
    return (
        output,
        grad_input,
        grad_gain_one,
        grad_w_query,
        grad_w_key,
        grad_w_value,
        grad_w_out,
        grad_gain_two,
        grad_w_gate,
        grad_w_up,
        grad_w_down,
    )


def solution(mesh):
    placed = (
        P("dp", None),
        P("dp"),
        P(),
        P(),
        P(None, "tensor"),
        P(None, "tensor"),
        P(None, "tensor"),
        P("tensor", None),
        P(),
        P(None, "tensor"),
        P(None, "tensor"),
        P("tensor", None),
        P("dp", None),
    )
    return jax.shard_map(
        on_device,
        mesh=mesh,
        in_specs=placed,
        out_specs=(
            P("dp", None),
            P("dp", None),
            P(),
            P(None, "tensor"),
            P(None, "tensor"),
            P(None, "tensor"),
            P("tensor", None),
            P(),
            P(None, "tensor"),
            P(None, "tensor"),
            P("tensor", None),
        ),
        check_vma=False,
    )
```

profile of v0, /device:TPU:0, one launch (start us, length us, event | category | flops | bytes accessed | tf_op | source)
XLA Modules:
  0.0 919.7 jit_solution(16879764175254552638)
XLA Ops:
  19.7 10.9 %all-gather = bf16[8,1,512]{2,1,0:T(2,128)(2,1)S(1)} all-gather(bf16[1,1,512]{2,1,0:T(2,128)(2,1)S(1)} %reshape.237), channel_id=1, replica_groups=mesh['dp'=8,'tensor'=4] {'dp'}, dimensions={0}, use_global_device_ids=true | all-gather | bytes 9216 | tf_op jit(solution)/shard_map/all_gather | solution.py:160
  30.7 3.7 fusion.102
  34.7 25.2 %all-gather.3.cloned.1.call-done = bf16[4096,512]{0,1:T(8,128)(2,1)} async-done(((bf16[512,512]{0,1:T(8,128)(2,1)}), bf16[4096,512]{0,1:T(8,128)(2,1)}) %all-gather.3.cloned.1.call-update) | async-done | bytes 4194320 | tf_op jit(solution)/shard_map/all_gather | solution.py:157
  59.9 4.7 fusion.110
  64.6 3.4 copy-done.10
  70.2 3.5 fusion.111
  75.0 3.7 fusion.112
  80.0 5.5 fusion.113
  86.8 7.1 fusion.38
  103.0 86.2 %all-reduce.5.cloned.1.call-done = bf16[512,2048]{1,0:T(8,128)(2,1)} async-done(((bf16[512,2048]{1,0:T(8,128)(2,1)}), bf16[512,2048]{1,0:T(8,128)(2,1)}) %all-reduce.5.cloned.1.call-update) | async-done | bytes 2097168 | tf_op jit(solution)/shard_map/psum | solution.py:175
  189.2 3.3 multiply_reduce_fusion.4
  193.7 8.9 fusion.115
  202.5 5.0 fusion.114
  207.5 7.5 multiply_convert_fusion.6
  215.0 3.4 fusion.116
  218.5 6.3 fusion.119
  224.8 4.6 add_convert_fusion.1
  229.7 5.4 fusion.42
  237.5 7.1 dynamic-slice_convert_fusion.1
  245.1 3.5 fusion.118
  248.6 4.4 copy-done.37
  254.9 4.6 convolution_convert_fusion.1
  259.5 55.2 %all-reduce.7.cloned.1.call-done = bf16[512,2048]{1,0:T(8,128)(2,1)} async-done(((bf16[512,2048]{1,0:T(8,128)(2,1)}), bf16[512,2048]{1,0:T(8,128)(2,1)}) %all-reduce.7.cloned.1.call-update) | async-done | bytes 2097168 | tf_op jit(solution)/shard_map/psum | solution.py:198
  314.8 4.9 fusion.19
  319.7 3.5 convert_add_fusion.4
  327.1 4.9 fusion.28
  332.0 3.6 fusion.25
  336.8 6.6 fusion.12
  343.4 4.6 fusion.13
  348.0 4.6 fusion.46
  352.6 4.5 fusion.48
  357.1 4.6 fusion.58
  361.8 20.2 %multiply_reduce_fusion.2 = (f32[512]{0:T(512)S(1)}, f32[512]{0:T(512)S(1)}, f32[512]{0:T(512)S(1)}, f32[512]{0:T(512)S(1)}, f32[512,4096]{1,0:T(8,128)}) fusion(f32[512,4096]{1,0:T(8,128)S(1)} %bitcast.53, f32[512]{0:T(512)S(1)} %get-tuple-element.97, s32[512]{0:T(512)S(1)} %copy-done.74, pred[4096]{0:T(1024)(128)(4,1)S(1)} %bitcast.95, ...), kind=kOutput, calls=%fused_computation.7 | convolution fusion | flops 578811904 | bytes 68329472 | tf_op jit(solution)/shard_map/dot_general | solution.py:42
  381.9 10.0 %multiply_convert_fusion = bf16[512,4096]{1,0:T(8,128)(2,1)} fusion(f32[512,4096]{1,0:T(8,128)} %fusion.46, f32[512]{0:T(512)S(1)} %get-tuple-element.18, f32[512,4096]{1,0:T(8,128)} %copy-done.10, f32[512]{0:T(512)S(1)} %get-tuple-element.95, s32[512]{0:T(512)S(1)} %copy-done.74, pred[4096]{0:T(1024)(128)(4,1)S(1)} %bitcast.96, s32[512]{0:T(512)S(1)} %copy-done.72, ...), kind=kLoop, calls=%fused_computation | loop fusion | flops 18874368 | bytes 21000192 | tf_op jit(solution)/shard_map/convert_element_type | solution.py:226
  391.9 18.2 %multiply_convert_fusion.2 = (bf16[512,4096]{1,0:T(8,128)(2,1)}, bf16[512,4096]{1,0:T(8,128)(2,1)}, bf16[512,4096]{1,0:T(8,128)(2,1)}) fusion(f32[512,4096]{1,0:T(8,128)} %get-tuple-element.94, f32[512]{0:T(512)S(1)} %get-tuple-element.15, f32[512,4096]{1,0:T(8,128)S(1)} %bitcast.53, f32[512]{0:T(512)S(1)} %get-tuple-element.97, s32[512]{0:T(512)S(1)} %copy-done.74, ...), kind=kLoop, calls=%fused_computation.6 | loop fusion | flops 39845888 | bytes 62951424 | tf_op jit(solution)/shard_map/convert_element_type | solution.py:226
  420.9 4.2 convolution_multiply_fusion.2
  443.3 5.0 convert_add_fusion.1
  451.2 4.2 convert_add_fusion.2
  462.2 4.0 convert_add_fusion.3
  466.2 68.0 %collective-permute-done.22 = bf16[512,512]{1,0:T(8,128)(2,1)} collective-permute-done((bf16[512,512]{1,0:T(8,128)(2,1)}, bf16[512,512]{1,0:T(8,128)(2,1)}, u32[]{:S(2)}, u32[]{:S(2)}) %collective-permute-start.22) | collective-permute-done | bytes 524320 | tf_op jit(solution)/shard_map/ppermute | solution.py:68
  537.0 8.2 collective-permute-done.4
  548.3 6.4 collective-permute-done.5
  556.3 4.0 collective-permute-done.24
  560.8 4.1 collective-permute-done.6
  571.7 10.6 %collective-permute-done.31 = bf16[512,1408]{1,0:T(8,128)(2,1)S(1)} collective-permute-done((bf16[512,1408]{1,0:T(8,128)(2,1)S(1)}, bf16[512,1408]{1,0:T(8,128)(2,1)S(1)}, u32[]{:S(2)}, u32[]{:S(2)}) %collective-permute-start.31) | collective-permute-done | bytes 1441824 | tf_op jit(solution)/shard_map/ppermute | solution.py:68
  584.3 9.3 %collective-permute-done.25 = bf16[512,512]{1,0:T(8,128)(2,1)S(1)} collective-permute-done((bf16[512,512]{1,0:T(8,128)(2,1)S(1)}, bf16[512,512]{1,0:T(8,128)(2,1)S(1)}, u32[]{:S(2)}, u32[]{:S(2)}) %collective-permute-start.25) | collective-permute-done | bytes 524320 | tf_op jit(solution)/shard_map/ppermute | solution.py:73
  594.0 9.3 %collective-permute-done.7 = bf16[512,512]{1,0:T(8,128)(2,1)S(1)} collective-permute-done((bf16[512,512]{1,0:T(8,128)(2,1)S(1)}, bf16[512,512]{1,0:T(8,128)(2,1)S(1)}, u32[]{:S(2)}, u32[]{:S(2)}) %collective-permute-start.7) | collective-permute-done | bytes 524320 | tf_op jit(solution)/shard_map/ppermute | solution.py:73
  606.3 11.1 %collective-permute-done.32 = bf16[256,1408]{1,0:T(8,128)(2,1)S(1)} collective-permute-done((bf16[256,1408]{1,0:T(8,128)(2,1)S(1)}, bf16[256,1408]{1,0:T(8,128)(2,1)S(1)}, u32[]{:S(2)}, u32[]{:S(2)}) %collective-permute-start.32) | collective-permute-done | bytes 720928 | tf_op jit(solution)/shard_map/ppermute | solution.py:68
  619.3 13.5 %collective-permute-done.45 = bf16[1408,256]{1,0:T(8,128)(2,1)S(1)} collective-permute-done((bf16[1408,256]{1,0:T(8,128)(2,1)S(1)}, bf16[1408,256]{1,0:T(8,128)(2,1)S(1)}, u32[]{:S(2)}, u32[]{:S(2)}) %collective-permute-start.45) | collective-permute-done | bytes 720928 | tf_op jit(solution)/shard_map/ppermute | solution.py:73
  634.8 13.5 %collective-permute-done.39 = bf16[256,1408]{1,0:T(8,128)(2,1)S(1)} collective-permute-done((bf16[256,1408]{1,0:T(8,128)(2,1)S(1)}, bf16[256,1408]{1,0:T(8,128)(2,1)S(1)}, u32[]{:S(2)}, u32[]{:S(2)}) %collective-permute-start.39) | collective-permute-done | bytes 720928 | tf_op jit(solution)/shard_map/ppermute | solution.py:73
  650.3 11.3 %collective-permute-done.33 = bf16[256,1408]{1,0:T(8,128)(2,1)S(1)} collective-permute-done((bf16[256,1408]{1,0:T(8,128)(2,1)S(1)}, bf16[256,1408]{1,0:T(8,128)(2,1)S(1)}, u32[]{:S(2)}, u32[]{:S(2)}) %collective-permute-start.33) | collective-permute-done | bytes 720928 | tf_op jit(solution)/shard_map/ppermute | solution.py:73
  672.4 26.1 %collective-permute-done.40 = bf16[512,1408]{1,0:T(8,128)(2,1)S(1)} collective-permute-done((bf16[512,1408]{1,0:T(8,128)(2,1)S(1)}, bf16[512,1408]{1,0:T(8,128)(2,1)S(1)}, u32[]{:S(2)}, u32[]{:S(2)}) %collective-permute-start.40) | collective-permute-done | bytes 1441824 | tf_op jit(solution)/shard_map/ppermute | solution.py:73
  701.0 23.3 %collective-permute-done.34 = bf16[512,1408]{1,0:T(8,128)(2,1)S(1)} collective-permute-done((bf16[512,1408]{1,0:T(8,128)(2,1)S(1)}, bf16[512,1408]{1,0:T(8,128)(2,1)S(1)}, u32[]{:S(2)}, u32[]{:S(2)}) %collective-permute-start.34) | collective-permute-done | bytes 1441824 | tf_op jit(solution)/shard_map/ppermute | solution.py:73
  745.1 5.5 collective-permute-done.10
  757.7 4.1 collective-permute-done.17
  768.5 4.6 collective-permute-done.13
  779.9 5.6 broadcast_select_fusion.3
  785.5 6.9 broadcast_select_fusion.5
  792.4 5.9 maximum_convert_fusion.2
  798.3 5.7 maximum_convert_fusion.1
  804.0 5.2 maximum_convert_fusion
  813.3 82.8 %all-reduce.9.cloned.1.call-done = (bf16[512,2048]{1,0:T(8,128)(2,1)}, bf16[512,2048]{1,0:T(8,128)(2,1)}) async-done(((bf16[512,2048]{1,0:T(8,128)(2,1)}, bf16[512,2048]{1,0:T(8,128)(2,1)}), (bf16[512,2048]{1,0:T(8,128)(2,1)}, bf16[512,2048]{1,0:T(8,128)(2,1)})) %all-reduce.9.cloned.1.call-update) | async-done | bytes 4194320 | tf_op jit(solution)/shard_map/psum | solution.py:185
  896.1 3.5 fusion.20
  906.3 6.2 fusion.21
  (432 shorter events, 168.7 us)
Async XLA Ops:
  7.2 93.1 %copy-start = (bf16[512,2048]{1,0:T(8,128)(2,1)S(1)}, bf16[512,2048]{1,0:T(8,128)(2,1)}, u32[]{:S(2)}) copy-start(bf16[512,2048]{1,0:T(8,128)(2,1)} %param.20) | copy-start | bytes 6291460
  7.2 52.7 %all-gather.3.cloned.1.call-start = ((), (), s32[]{:S(2)}) async-start(), calls=%async_computation.1 | async-start | bytes 4718592 | tf_op jit(solution)/shard_map/all_gather | solution.py:157
  11.8 68.2 %copy-start.63 = (s32[2,2,8,128]{3,1,2,0:T(2,128)}, s32[2,2,8,128]{3,1,2,0:T(2,128)S(1)}, u32[]{:S(2)}) copy-start(s32[2,2,8,128]{3,1,2,0:T(2,128)S(1)} %copy.24) | copy-start | bytes 49156
  16.4 63.6 %copy-start.71 = (s32[512]{0:T(512)}, s32[512]{0:T(512)S(1)}, u32[]{:S(2)}) copy-start(s32[512]{0:T(512)S(1)} %get-tuple-element.22) | copy-start | bytes 6148
  19.6 169.5 %all-reduce.5.cloned.1.call-start = ((), (), s32[]{:S(2)}) async-start(), calls=%async_computation.2 | async-start | bytes 4194304 | tf_op jit(solution)/shard_map/psum | solution.py:175
  19.7 304.9 %copy-start.65 = (f32[512]{0:T(512)}, f32[512]{0:T(512)S(1)}, u32[]{:S(2)}) copy-start(f32[512]{0:T(512)S(1)} %get-tuple-element.84) | copy-start | bytes 6148
  30.7 49.3 %copy-start.67 = (pred[1,4,8,128]{3,1,2,0:T(4,128)(4,1)}, pred[1,4,8,128]{3,1,2,0:T(4,128)(4,1)S(1)}, u32[]{:S(2)}) copy-start(pred[1,4,8,128]{3,1,2,0:T(4,128)(4,1)S(1)} %copy.25) | copy-start | bytes 12292
  30.7 49.3 %copy-start.73 = (s32[512]{0:T(512)}, s32[512]{0:T(512)S(1)}, u32[]{:S(2)}) copy-start(s32[512]{0:T(512)S(1)} %iota_add_fusion) | copy-start | bytes 6148
  34.7 45.3 %copy-start.46 = (bf16[512,4,128]{0,2,1:T(8,128)(2,1)}, bf16[512,4,128]{0,2,1:T(8,128)(2,1)S(1)}, u32[]{:S(2)}) copy-start(bf16[512,4,128]{0,2,1:T(8,128)(2,1)S(1)} %pad_maximum_fusion.10) | copy-start | bytes 1572868
  102.9 211.9 %all-reduce.7.cloned.1.call-start = ((), (), s32[]{:S(2)}) async-start(), calls=%async_computation.3 | async-start | bytes 4194304 | tf_op jit(solution)/shard_map/psum | solution.py:198
  229.5 498.4 %reduce-scatter.2.cloned.1.call-start = ((), (), s32[]{:S(2)}) async-start(), calls=%async_computation.4 | async-start | bytes 4718592 | tf_op jit(solution)/shard_map/reduce_scatter | solution.py:236
  237.5 205.8 %collective-permute-start.42 = (bf16[1408,1024]{1,0:T(8,128)(2,1)}, bf16[1408,1024]{1,0:T(8,128)(2,1)}, u32[]{:S(2)}, u32[]{:S(2)}) collective-permute-start(bf16[1408,1024]{1,0:T(8,128)(2,1)} %dynamic-slice_convert_fusion), channel_id=1, source_target_pairs={{0,4},{4,0},{8,12},{12,8},{16,20},{20,16},{24,28},{28,24},{1,5},{5... | collective-permute-start | bytes 8650760 | tf_op jit(solution)/shard_map/ppermute | solution.py:68
  244.6 206.6 %collective-permute-start.36 = (bf16[1024,1408]{1,0:T(8,128)(2,1)}, bf16[1024,1408]{1,0:T(8,128)(2,1)}, u32[]{:S(2)}, u32[]{:S(2)}) collective-permute-start(bf16[1024,1408]{1,0:T(8,128)(2,1)} %dynamic-slice_convert_fusion.1), channel_id=1, source_target_pairs={{0,4},{4,0},{8,12},{12,8},{16,20},{20,16},{24,28},{28,24},{1,5},{5... | collective-permute-start | bytes 8650760 | tf_op jit(solution)/shard_map/ppermute | solution.py:68
  254.9 207.3 %collective-permute-start.30 = (bf16[1024,1408]{1,0:T(8,128)(2,1)}, bf16[1024,1408]{1,0:T(8,128)(2,1)}, u32[]{:S(2)}, u32[]{:S(2)}) collective-permute-start(bf16[1024,1408]{1,0:T(8,128)(2,1)} %dynamic-slice_convert_fusion.2), channel_id=1, source_target_pairs={{0,4},{4,0},{8,12},{12,8},{16,20},{20,16},{24,28},{28,24},{1,5},{5... | collective-permute-start | bytes 8650760 | tf_op jit(solution)/shard_map/ppermute | solution.py:68
  326.0 108.6 %collective-permute-start.27 = (f32[2048]{0:T(1024)S(1)}, f32[2048]{0:T(1024)}, u32[]{:S(2)}, u32[]{:S(2)}) collective-permute-start(f32[2048]{0:T(1024)S(1)} %get-tuple-element.11), channel_id=1, source_target_pairs={{0,4},{4,0},{8,12},{12,8},{16,20},{20,16},{24,28},{28,24},{1,5},{5... | collective-permute-start | bytes 24584 | tf_op jit(solution)/shard_map/ppermute | solution.py:87
  336.8 120.4 %collective-permute-start.21 = (bf16[512,1024]{1,0:T(8,128)(2,1)}, bf16[512,1024]{1,0:T(8,128)(2,1)}, u32[]{:S(2)}, u32[]{:S(2)}) collective-permute-start(bf16[512,1024]{1,0:T(8,128)(2,1)} %dynamic-slice_convert_fusion.6), channel_id=1, source_target_pairs={{0,4},{4,0},{8,12},{12,8},{16,20},{20,16},{24,28},{28,24},{1,5},{5... | collective-permute-start | bytes 3145736 | tf_op jit(solution)/shard_map/ppermute | solution.py:68
  420.6 475.5 %all-reduce.9.cloned.1.call-start = ((), (), s32[]{:S(2)}) async-start(), calls=%async_computation.5 | async-start | bytes 8388608 | tf_op jit(solution)/shard_map/psum | solution.py:185
  435.4 3.7 collective-permute-start.28
  439.0 3.7 collective-permute-start.29
  442.7 18.6 %collective-permute-start.3 = (bf16[1024,512]{1,0:T(8,128)(2,1)S(1)}, bf16[1024,512]{1,0:T(8,128)(2,1)S(1)}, u32[]{:S(2)}, u32[]{:S(2)}) collective-permute-start(bf16[1024,512]{1,0:T(8,128)(2,1)S(1)} %dynamic-slice_convert_fusion.7), channel_id=1, source_target_pairs={{0,4},{4,0},{8,12},{12,8},{16,20},{20,16},{24,28},{28,24},{1,5},{5... | collective-permute-start | bytes 3145736 | tf_op jit(solution)/shard_map/ppermute | solution.py:68
  449.6 115.8 %collective-permute-start.43 = (bf16[1408,512]{1,0:T(8,128)(2,1)}, bf16[1408,512]{1,0:T(8,128)(2,1)}, u32[]{:S(2)}, u32[]{:S(2)}) collective-permute-start(bf16[1408,512]{1,0:T(8,128)(2,1)} %dynamic-slice_convert_fusion.3), channel_id=1, source_target_pairs={{0,8},{4,12},{8,0},{12,4},{16,24},{20,28},{24,16},{28,20},{1,9},{5... | collective-permute-start | bytes 4325384 | tf_op jit(solution)/shard_map/ppermute | solution.py:68
  456.7 112.5 %collective-permute-start.37 = (bf16[512,1408]{1,0:T(8,128)(2,1)}, bf16[512,1408]{1,0:T(8,128)(2,1)}, u32[]{:S(2)}, u32[]{:S(2)}) collective-permute-start(bf16[512,1408]{1,0:T(8,128)(2,1)} %dynamic-slice_convert_fusion.4), channel_id=1, source_target_pairs={{0,8},{4,12},{8,0},{12,4},{16,24},{20,28},{24,16},{28,20},{1,9},{5... | collective-permute-start | bytes 4325384 | tf_op jit(solution)/shard_map/ppermute | solution.py:68
  459.7 74.5 %collective-permute-start.22 = (bf16[512,512]{1,0:T(8,128)(2,1)}, bf16[512,512]{1,0:T(8,128)(2,1)}, u32[]{:S(2)}, u32[]{:S(2)}) collective-permute-start(bf16[512,512]{1,0:T(8,128)(2,1)} %dynamic-slice_convert_fusion.11), channel_id=1, source_target_pairs={{0,8},{4,12},{8,0},{12,4},{16,24},{20,28},{24,16},{28,20},{1,9},{5... | collective-permute-start | bytes 1572872 | tf_op jit(solution)/shard_map/ppermute | solution.py:68
  461.7 83.5 %collective-permute-start.4 = (bf16[512,512]{1,0:T(8,128)(2,1)S(1)}, bf16[512,512]{1,0:T(8,128)(2,1)S(1)}, u32[]{:S(2)}, u32[]{:S(2)}) collective-permute-start(bf16[512,512]{1,0:T(8,128)(2,1)S(1)} %dynamic-slice_convert_fusion.14), channel_id=1, source_target_pairs={{0,8},{4,12},{8,0},{12,4},{16,24},{20,28},{24,16},{28,20},{1,9},{5... | collective-permute-start | bytes 1572872 | tf_op jit(solution)/shard_map/ppermute | solution.py:68
  535.5 11.5 %collective-permute-start.23 = (bf16[512,256]{1,0:T(8,128)(2,1)S(1)}, bf16[512,256]{1,0:T(8,128)(2,1)S(1)}, u32[]{:S(2)}, u32[]{:S(2)}) collective-permute-start(bf16[512,256]{1,0:T(8,128)(2,1)S(1)} %dynamic-slice_convert_fusion.15), channel_id=1, source_target_pairs={{0,16},{4,20},{8,24},{12,28},{16,0},{20,4},{24,8},{28,12},{1,17},{... | collective-permute-start | bytes 786440 | tf_op jit(solution)/shard_map/ppermute | solution.py:68
  545.4 9.2 %collective-permute-start.5 = (bf16[256,512]{1,0:T(8,128)(2,1)S(1)}, bf16[256,512]{1,0:T(8,128)(2,1)S(1)}, u32[]{:S(2)}, u32[]{:S(2)}) collective-permute-start(bf16[256,512]{1,0:T(8,128)(2,1)S(1)} %dynamic-slice_convert_fusion.18), channel_id=1, source_target_pairs={{0,16},{4,20},{8,24},{12,28},{16,0},{20,4},{24,8},{28,12},{1,17},{... | collective-permute-start | bytes 786440 | tf_op jit(solution)/shard_map/ppermute | solution.py:68
  547.1 13.2 %collective-permute-start.24 = (bf16[512,256]{1,0:T(8,128)(2,1)S(1)}, bf16[512,256]{1,0:T(8,128)(2,1)S(1)}, u32[]{:S(2)}, u32[]{:S(2)}) collective-permute-start(bf16[512,256]{1,0:T(8,128)(2,1)S(1)} %add_convert_fusion.6), channel_id=1, source_target_pairs={{0,16},{4,20},{8,24},{12,28},{16,0},{20,4},{24,8},{28,12},{1,17},{... | collective-permute-start | bytes 786440 | tf_op jit(solution)/shard_map/ppermute | solution.py:73
  547.9 34.5 %collective-permute-start.31 = (bf16[512,1408]{1,0:T(8,128)(2,1)S(1)}, bf16[512,1408]{1,0:T(8,128)(2,1)S(1)}, u32[]{:S(2)}, u32[]{:S(2)}) collective-permute-start(bf16[512,1408]{1,0:T(8,128)(2,1)S(1)} %dynamic-slice_convert_fusion.5), channel_id=1, source_target_pairs={{0,8},{4,12},{8,0},{12,4},{16,24},{20,28},{24,16},{28,20},{1,9},{5... | collective-permute-start | bytes 4325384 | tf_op jit(solution)/shard_map/ppermute | solution.py:68
  554.8 10.2 %collective-permute-start.6 = (bf16[256,512]{1,0:T(8,128)(2,1)S(1)}, bf16[256,512]{1,0:T(8,128)(2,1)S(1)}, u32[]{:S(2)}, u32[]{:S(2)}) collective-permute-start(bf16[256,512]{1,0:T(8,128)(2,1)S(1)} %add_convert_fusion.7), channel_id=1, source_target_pairs={{0,16},{4,20},{8,24},{12,28},{16,0},{20,4},{24,8},{28,12},{1,17},{... | collective-permute-start | bytes 786440 | tf_op jit(solution)/shard_map/ppermute | solution.py:73
  560.4 33.2 %collective-permute-start.25 = (bf16[512,512]{1,0:T(8,128)(2,1)S(1)}, bf16[512,512]{1,0:T(8,128)(2,1)S(1)}, u32[]{:S(2)}, u32[]{:S(2)}) collective-permute-start(bf16[512,512]{1,0:T(8,128)(2,1)S(1)} %pad_maximum_fusion.17), channel_id=1, source_target_pairs={{0,8},{4,12},{8,0},{12,4},{16,24},{20,28},{24,16},{28,20},{1,9},{5... | collective-permute-start | bytes 1572872 | tf_op jit(solution)/shard_map/ppermute | solution.py:73
  565.0 38.3 %collective-permute-start.7 = (bf16[512,512]{1,0:T(8,128)(2,1)S(1)}, bf16[512,512]{1,0:T(8,128)(2,1)S(1)}, u32[]{:S(2)}, u32[]{:S(2)}) collective-permute-start(bf16[512,512]{1,0:T(8,128)(2,1)S(1)} %pad_maximum_fusion.14), channel_id=1, source_target_pairs={{0,8},{4,12},{8,0},{12,4},{16,24},{20,28},{24,16},{28,20},{1,9},{5... | collective-permute-start | bytes 1572872 | tf_op jit(solution)/shard_map/ppermute | solution.py:73
  567.4 36.3 %collective-permute-start.44 = (bf16[1408,256]{1,0:T(8,128)(2,1)S(1)}, bf16[1408,256]{1,0:T(8,128)(2,1)S(1)}, u32[]{:S(2)}, u32[]{:S(2)}) collective-permute-start(bf16[1408,256]{1,0:T(8,128)(2,1)S(1)} %dynamic-slice_convert_fusion.8), channel_id=1, source_target_pairs={{0,16},{4,20},{8,24},{12,28},{16,0},{20,4},{24,8},{28,12},{1,17},{... | collective-permute-start | bytes 2162696 | tf_op jit(solution)/shard_map/ppermute | solution.py:68
  571.4 34.2 %collective-permute-start.38 = (bf16[256,1408]{1,0:T(8,128)(2,1)S(1)}, bf16[256,1408]{1,0:T(8,128)(2,1)S(1)}, u32[]{:S(2)}, u32[]{:S(2)}) collective-permute-start(bf16[256,1408]{1,0:T(8,128)(2,1)S(1)} %dynamic-slice_convert_fusion.9), channel_id=1, source_target_pairs={{0,16},{4,20},{8,24},{12,28},{16,0},{20,4},{24,8},{28,12},{1,17},{... | collective-permute-start | bytes 2162696 | tf_op jit(solution)/shard_map/ppermute | solution.py:68
  582.8 34.6 %collective-permute-start.32 = (bf16[256,1408]{1,0:T(8,128)(2,1)S(1)}, bf16[256,1408]{1,0:T(8,128)(2,1)S(1)}, u32[]{:S(2)}, u32[]{:S(2)}) collective-permute-start(bf16[256,1408]{1,0:T(8,128)(2,1)S(1)} %dynamic-slice_convert_fusion.10), channel_id=1, source_target_pairs={{0,16},{4,20},{8,24},{12,28},{16,0},{20,4},{24,8},{28,12},{1,17},{... | collective-permute-start | bytes 2162696 | tf_op jit(solution)/shard_map/ppermute | solution.py:68
  593.9 69.7 %collective-permute-start.26 = (bf16[512,1024]{1,0:T(8,128)(2,1)S(1)}, bf16[512,1024]{1,0:T(8,128)(2,1)S(1)}, u32[]{:S(2)}, u32[]{:S(2)}) collective-permute-start(bf16[512,1024]{1,0:T(8,128)(2,1)S(1)} %pad_maximum_fusion.9), channel_id=1, source_target_pairs={{0,4},{4,0},{8,12},{12,8},{16,20},{20,16},{24,28},{28,24},{1,5},{5... | collective-permute-start | bytes 3145736 | tf_op jit(solution)/shard_map/ppermute | solution.py:73
  603.6 63.1 %collective-permute-start.8 = (bf16[1024,512]{1,0:T(8,128)(2,1)S(1)}, bf16[1024,512]{1,0:T(8,128)(2,1)S(1)}, u32[]{:S(2)}, u32[]{:S(2)}) collective-permute-start(bf16[1024,512]{1,0:T(8,128)(2,1)S(1)} %pad_maximum_fusion.8), channel_id=1, source_target_pairs={{0,4},{4,0},{8,12},{12,8},{16,20},{20,16},{24,28},{28,24},{1,5},{5... | collective-permute-start | bytes 3145736 | tf_op jit(solution)/shard_map/ppermute | solution.py:73
  604.0 28.8 %collective-permute-start.45 = (bf16[1408,256]{1,0:T(8,128)(2,1)S(1)}, bf16[1408,256]{1,0:T(8,128)(2,1)S(1)}, u32[]{:S(2)}, u32[]{:S(2)}) collective-permute-start(bf16[1408,256]{1,0:T(8,128)(2,1)S(1)} %add_convert_fusion.3), channel_id=1, source_target_pairs={{0,16},{4,20},{8,24},{12,28},{16,0},{20,4},{24,8},{28,12},{1,17},{... | collective-permute-start | bytes 2162696 | tf_op jit(solution)/shard_map/ppermute | solution.py:73
  605.7 42.6 %collective-permute-start.39 = (bf16[256,1408]{1,0:T(8,128)(2,1)S(1)}, bf16[256,1408]{1,0:T(8,128)(2,1)S(1)}, u32[]{:S(2)}, u32[]{:S(2)}) collective-permute-start(bf16[256,1408]{1,0:T(8,128)(2,1)S(1)} %add_convert_fusion.4), channel_id=1, source_target_pairs={{0,16},{4,20},{8,24},{12,28},{16,0},{20,4},{24,8},{28,12},{1,17},{... | collective-permute-start | bytes 2162696 | tf_op jit(solution)/shard_map/ppermute | solution.py:73
  617.5 44.1 %collective-permute-start.33 = (bf16[256,1408]{1,0:T(8,128)(2,1)S(1)}, bf16[256,1408]{1,0:T(8,128)(2,1)S(1)}, u32[]{:S(2)}, u32[]{:S(2)}) collective-permute-start(bf16[256,1408]{1,0:T(8,128)(2,1)S(1)} %add_convert_fusion.5), channel_id=1, source_target_pairs={{0,16},{4,20},{8,24},{12,28},{16,0},{20,4},{24,8},{28,12},{1,17},{... | collective-permute-start | bytes 2162696 | tf_op jit(solution)/shard_map/ppermute | solution.py:73
  633.1 36.7 %collective-permute-start.46 = (bf16[1408,512]{1,0:T(8,128)(2,1)S(1)}, bf16[1408,512]{1,0:T(8,128)(2,1)S(1)}, u32[]{:S(2)}, u32[]{:S(2)}) collective-permute-start(bf16[1408,512]{1,0:T(8,128)(2,1)S(1)} %pad_maximum_fusion.6), channel_id=1, source_target_pairs={{0,8},{4,12},{8,0},{12,4},{16,24},{20,28},{24,16},{28,20},{1,9},{5... | collective-permute-start | bytes 4325384 | tf_op jit(solution)/shard_map/ppermute | solution.py:73
  648.6 49.9 %collective-permute-start.40 = (bf16[512,1408]{1,0:T(8,128)(2,1)S(1)}, bf16[512,1408]{1,0:T(8,128)(2,1)S(1)}, u32[]{:S(2)}, u32[]{:S(2)}) collective-permute-start(bf16[512,1408]{1,0:T(8,128)(2,1)S(1)} %pad_maximum_fusion.5), channel_id=1, source_target_pairs={{0,8},{4,12},{8,0},{12,4},{16,24},{20,28},{24,16},{28,20},{1,9},{5... | collective-permute-start | bytes 4325384 | tf_op jit(solution)/shard_map/ppermute | solution.py:73
  661.9 62.4 %collective-permute-start.34 = (bf16[512,1408]{1,0:T(8,128)(2,1)S(1)}, bf16[512,1408]{1,0:T(8,128)(2,1)S(1)}, u32[]{:S(2)}, u32[]{:S(2)}) collective-permute-start(bf16[512,1408]{1,0:T(8,128)(2,1)S(1)} %pad_maximum_fusion.4), channel_id=1, source_target_pairs={{0,8},{4,12},{8,0},{12,4},{16,24},{20,28},{24,16},{28,20},{1,9},{5... | collective-permute-start | bytes 4325384 | tf_op jit(solution)/shard_map/ppermute | solution.py:73
  670.4 28.7 %copy-start.23 = (bf16[1408,512]{1,0:T(8,128)(2,1)}, bf16[1408,512]{1,0:T(8,128)(2,1)S(1)}, u32[]{:S(2)}) copy-start(bf16[1408,512]{1,0:T(8,128)(2,1)S(1)} %get-tuple-element.33) | copy-start | bytes 4325380
  672.4 104.5 %collective-permute-start.47 = (bf16[1408,1024]{1,0:T(8,128)(2,1)}, bf16[1408,1024]{1,0:T(8,128)(2,1)}, u32[]{:S(2)}, u32[]{:S(2)}) collective-permute-start(bf16[1408,1024]{1,0:T(8,128)(2,1)} %pad_maximum_fusion.3), channel_id=1, source_target_pairs={{0,4},{4,0},{8,12},{12,8},{16,20},{20,16},{24,28},{28,24},{1,5},{5... | collective-permute-start | bytes 8650760 | tf_op jit(solution)/shard_map/ppermute | solution.py:73
  701.0 78.8 %collective-permute-start.41 = (bf16[1024,1408]{1,0:T(8,128)(2,1)}, bf16[1024,1408]{1,0:T(8,128)(2,1)}, u32[]{:S(2)}, u32[]{:S(2)}) collective-permute-start(bf16[1024,1408]{1,0:T(8,128)(2,1)} %pad_maximum_fusion.2), channel_id=1, source_target_pairs={{0,4},{4,0},{8,12},{12,8},{16,20},{20,16},{24,28},{28,24},{1,5},{5... | collective-permute-start | bytes 8650760 | tf_op jit(solution)/shard_map/ppermute | solution.py:73
  727.8 57.6 %collective-permute-start.35 = (bf16[1024,1408]{1,0:T(8,128)(2,1)}, bf16[1024,1408]{1,0:T(8,128)(2,1)}, u32[]{:S(2)}, u32[]{:S(2)}) collective-permute-start(bf16[1024,1408]{1,0:T(8,128)(2,1)} %pad_maximum_fusion.1), channel_id=1, source_target_pairs={{0,4},{4,0},{8,12},{12,8},{16,20},{20,16},{24,28},{28,24},{1,5},{5... | collective-permute-start | bytes 8650760 | tf_op jit(solution)/shard_map/ppermute | solution.py:73
  732.8 7.0 collective-permute-start.9
  735.8 7.4 collective-permute-start.15
  741.4 9.2 %collective-permute-start.10 = (bf16[512,256]{1,0:T(8,128)(2,1)S(1)}, bf16[512,256]{1,0:T(8,128)(2,1)S(1)}, u32[]{:S(2)}, u32[]{:S(2)}) collective-permute-start(bf16[512,256]{1,0:T(8,128)(2,1)S(1)} %dynamic-slice_convert_fusion.17), channel_id=1, source_target_pairs={{0,8},{4,12},{8,0},{12,4},{16,24},{20,28},{24,16},{28,20},{1,9},{5... | collective-permute-start | bytes 786440 | tf_op jit(solution)/shard_map/ppermute | solution.py:68
  744.7 10.7 %collective-permute-start.16 = (bf16[512,256]{1,0:T(8,128)(2,1)S(1)}, bf16[512,256]{1,0:T(8,128)(2,1)S(1)}, u32[]{:S(2)}, u32[]{:S(2)}) collective-permute-start(bf16[512,256]{1,0:T(8,128)(2,1)S(1)} %dynamic-slice_convert_fusion.16), channel_id=1, source_target_pairs={{0,8},{4,12},{8,0},{12,4},{16,24},{20,28},{24,16},{28,20},{1,9},{5... | collective-permute-start | bytes 786440 | tf_op jit(solution)/shard_map/ppermute | solution.py:68
  750.8 26.1 %copy-start.24 = (bf16[1408,512]{1,0:T(8,128)(2,1)S(1)}, bf16[1408,512]{1,0:T(8,128)(2,1)}, u32[]{:S(2)}) copy-start(bf16[1408,512]{1,0:T(8,128)(2,1)} %copy-done.23) | copy-start | bytes 4325380
  750.8 6.5 collective-permute-start.11
  755.5 6.3 collective-permute-start.17
  757.3 7.3 collective-permute-start.12
  761.9 5.0 collective-permute-start.18
  764.7 8.5 collective-permute-start.13
  766.9 9.0 collective-permute-start.19
  774.1 35.1 %collective-permute-start.14 = (bf16[1024,256]{1,0:T(8,128)(2,1)}, bf16[1024,256]{1,0:T(8,128)(2,1)}, u32[]{:S(2)}, u32[]{:S(2)}) collective-permute-start(bf16[1024,256]{1,0:T(8,128)(2,1)} %pad_maximum_fusion.15), channel_id=1, source_target_pairs={{0,4},{4,0},{8,12},{12,8},{16,20},{20,16},{24,28},{28,24},{1,5},{5... | collective-permute-start | bytes 1572872 | tf_op jit(solution)/shard_map/ppermute | solution.py:73
  776.9 33.6 %collective-permute-start.20 = (bf16[1024,256]{1,0:T(8,128)(2,1)}, bf16[1024,256]{1,0:T(8,128)(2,1)}, u32[]{:S(2)}, u32[]{:S(2)}) collective-permute-start(bf16[1024,256]{1,0:T(8,128)(2,1)} %pad_maximum_fusion.16), channel_id=1, source_target_pairs={{0,4},{4,0},{8,12},{12,8},{16,20},{20,16},{24,28},{28,24},{1,5},{5... | collective-permute-start | bytes 1572872 | tf_op jit(solution)/shard_map/ppermute | solution.py:73
  813.3 89.3 %copy-start.76 = (f32[512]{0:T(512)S(1)}, f32[512]{0:T(512)}, u32[]{:S(2)}) copy-start(f32[512]{0:T(512)} %copy-done.75) | copy-start | bytes 6148
  813.3 93.0 %copy-start.66 = (f32[512]{0:T(512)S(1)}, f32[512]{0:T(512)}, u32[]{:S(2)}) copy-start(f32[512]{0:T(512)} %copy-done.65) | copy-start | bytes 6148
  899.5 1.6 collective-permute-start
  901.1 3.7 collective-permute-start.1
  904.8 7.7 collective-permute-start.2
  (87 other events, 619.4 us)
Sparse Core Ops, SparseCore 0:
  19.8 40.0 all-gather.2
  103.0 86.1 all-reduce.4
  229.6 85.1 all-reduce.6
  420.7 59.7 reduce-scatter.1
  740.0 156.0 all-reduce.8
where the time goes:
time: 924 us; the launch traced here: 920 us
  waiting for transfers between devices  494 us (53%)
  matrix products  174 us (19%)
  other arithmetic  148 us (16%)
  starting transfers between devices  42.3 us (5%)
  local copies, waits for them, and re-layouts  35.2 us (4%)
  between operations  15.7 us (2%)
  blocking collectives  10.9 us (1%)
    ppermute x21, waiting for transfers between devices, permute_sum(): got = lax.ppermute(pieces, axis, partner_perm(size, 1 << step))  123 us
    ppermute x21, waiting for transfers between devices, permute_sum(): got = lax.ppermute(send, axis, partner_perm(size, 1 << step))  117 us
    psum x1, waiting for transfers between devices, on_device(): lax.psum(jnp.dot(attended, w_out, preferred_element_type=jnp.float32).ast...  86.2 us
    psum x1, waiting for transfers between devices, on_device(): lax.psum(jnp.dot(hidden, w_down, preferred_element_type=jnp.float32).asty...  82.8 us
    dot_general x15, matrix products, right_trans(): lax.dot_general(left, right, (((1,), (1,)), ((), ())), preferred_element_...  72.6 us
    psum x1, waiting for transfers between devices, on_device(): lax.psum((right_trans(d_gate, w_gate) + right_trans(d_up, w_up)).astype(j...  55.2 us
    dot_general x15, matrix products, left_trans(): lax.dot_general(left, right, (((0,), (0,)), ((), ())), preferred_element_...  45.3 us
    convert_element_type x2, other arithmetic, on_device(): d_scores = (probs * (d_probs - row_delta)).astype(jnp.bfloat16)  28.1 us
  transfers between devices with their start and end apart: 53, of which 28 were waited for; matrix products, arithmetic and copies ran while one was open for 27% of the time, Pallas kernels for 0%

commit v1 on v0

--- a/solution.py
+++ b/solution.py
@@ -1,3 +1,4 @@
+import functools
 import jax
 import jax.numpy as jnp
 from jax import lax
@@ -6,6 +7,13 @@
 HEAD_DIM = 128
 EPS = 1e-05
 MASKED_SCORE = -1e30
+
+
+def note_the_vector(view, across):
+    return jnp.sum(lax.all_gather(view, across), 0)
+
+
+finish_view = functools.partial(note_the_vector, across="tensor")
 
 
 def rms_norm(values, scales):
@@ -195,8 +203,8 @@
     d_up = d_up_full.astype(jnp.bfloat16)
     grad_w_gate = left_trans(normed_two, d_gate)
     grad_w_up = left_trans(normed_two, d_up)
-    d_normed_two = lax.psum(
-        (right_trans(d_gate, w_gate) + right_trans(d_up, w_up)).astype(jnp.bfloat16), "tensor"
+    d_normed_two = finish_view(
+        (right_trans(d_gate, w_gate) + right_trans(d_up, w_up)).astype(jnp.bfloat16)
     ).astype(jnp.float32)
     d_middle_norm, grad_gain_two = norm_two_back(d_normed_two)
     grad_middle = grad_out + d_middle_norm

time: 924 us -> 882 us (0.955)
  waiting for transfers between devices: 494 us -> 460 us
  matrix products: 174 us -> 162 us
    psum x1 -> x0, waiting for transfers between devices: 55.2 us -> none  [on_device(): lax.psum((right_trans(d_gate, w_gate) + right_trans(d_up, w_up)).astype(j...]
    psum x1, waiting for transfers between devices: 82.8 us -> 114 us  [on_device(): lax.psum(jnp.dot(hidden, w_down, preferred_element_type=jnp.float32).asty...]
    ppermute x21, waiting for transfers between devices: 123 us -> 108 us  [permute_sum(): got = lax.ppermute(pieces, axis, partner_perm(size, 1 << step))]
    unnamed x199 -> x219, local copies, waits for them, and re-layouts: 15.7 us -> 24.1 us
  transfers between devices with their start and end apart: 53 -> 53, of which waited for: 28 -> 25; matrix products, arithmetic and copies ran while one was open for 27% -> 27% of each run, Pallas kernels for 0% -> 0%
where the time goes in v1:
time: 882 us; the launch traced here: 879 us
  waiting for transfers between devices  460 us (52%)
  matrix products  162 us (18%)
  other arithmetic  148 us (17%)
  starting transfers between devices  46.1 us (5%)
  local copies, waits for them, and re-layouts  36.7 us (4%)
  between operations  16.1 us (2%)
  blocking collectives  10.6 us (1%)
    ppermute x21, waiting for transfers between devices, permute_sum(): got = lax.ppermute(send, axis, partner_perm(size, 1 << step))  125 us
    psum x1, waiting for transfers between devices, on_device(): lax.psum(jnp.dot(hidden, w_down, preferred_element_type=jnp.float32).asty...  114 us
    ppermute x21, waiting for transfers between devices, permute_sum(): got = lax.ppermute(pieces, axis, partner_perm(size, 1 << step))  108 us
    psum x1, waiting for transfers between devices, on_device(): lax.psum(jnp.dot(attended, w_out, preferred_element_type=jnp.float32).ast...  85 us
    dot_general x15, matrix products, right_trans(): lax.dot_general(left, right, (((1,), (1,)), ((), ())), preferred_element_...  73.2 us
    dot_general x15, matrix products, left_trans(): lax.dot_general(left, right, (((0,), (0,)), ((), ())), preferred_element_...  40.5 us
    convert_element_type x2, other arithmetic, on_device(): d_scores = (probs * (d_probs - row_delta)).astype(jnp.bfloat16)  29.1 us
    all_gather x1, waiting for transfers between devices, on_device(): lax.all_gather(jnp.concatenate([key_low, value_low], axis=1), 'dp', axis=...  25.4 us
  transfers between devices with their start and end apart: 53, of which 25 were waited for; matrix products, arithmetic and copies ran while one was open for 27% of the time, Pallas kernels for 0%

profile of v1, /device:TPU:0, one launch (start us, length us, event | category | flops | bytes accessed | tf_op | source)
XLA Modules:
  0.0 878.5 jit_solution(15628225776859118273)
XLA Ops:
  19.8 10.6 %all-gather.1 = bf16[8,1,512]{2,1,0:T(2,128)(2,1)S(1)} all-gather(bf16[1,1,512]{2,1,0:T(2,128)(2,1)S(1)} %reshape.238), channel_id=1, replica_groups=mesh['dp'=8,'tensor'=4] {'dp'}, dimensions={0}, use_global_device_ids=true | all-gather | bytes 9216 | tf_op jit(solution)/shard_map/all_gather | solution.py:168
  30.5 3.7 fusion.102
  34.5 25.4 %all-gather.5.cloned.1.call-done = bf16[4096,512]{0,1:T(8,128)(2,1)} async-done(((bf16[512,512]{0,1:T(8,128)(2,1)}), bf16[4096,512]{0,1:T(8,128)(2,1)}) %all-gather.5.cloned.1.call-update) | async-done | bytes 4194320 | tf_op jit(solution)/shard_map/all_gather | solution.py:165
  59.9 4.7 fusion.110
  64.6 3.4 copy-done.10
  70.2 3.5 fusion.111
  75.0 4.0 fusion.112
  80.3 5.5 fusion.113
  87.1 7.1 fusion.38
  104.9 85.0 %all-reduce.4.cloned.1.call-done = bf16[512,2048]{1,0:T(8,128)(2,1)} async-done(((bf16[512,2048]{1,0:T(8,128)(2,1)}), bf16[512,2048]{1,0:T(8,128)(2,1)}) %all-reduce.4.cloned.1.call-update) | async-done | bytes 2097168 | tf_op jit(solution)/shard_map/psum | solution.py:183
  189.9 3.3 multiply_reduce_fusion.4
  194.9 8.1 fusion.115
  203.0 5.0 fusion.114
  208.0 6.8 multiply_convert_fusion.6
  214.8 3.3 fusion.42
  223.5 3.5 fusion.119
  232.3 3.5 fusion.118
  235.8 4.4 copy-done.29
  242.1 3.8 fusion.116
  246.0 4.6 add_convert_fusion.1
  250.7 5.0 convert_add_fusion.1
  257.5 4.9 convert_add_fusion.2
  263.4 4.0 convert_add_fusion.3
  269.0 21.5 %collective-permute-done.43 = bf16[1408,512]{1,0:T(8,128)(2,1)S(1)} collective-permute-done((bf16[1408,512]{1,0:T(8,128)(2,1)S(1)}, bf16[1408,512]{1,0:T(8,128)(2,1)S(1)}, u32[]{:S(2)}, u32[]{:S(2)}) %collective-permute-start.43) | collective-permute-done | bytes 1441824 | tf_op jit(solution)/shard_map/ppermute | solution.py:76
  292.6 28.8 %collective-permute-done.37 = bf16[512,1408]{1,0:T(8,128)(2,1)S(1)} collective-permute-done((bf16[512,1408]{1,0:T(8,128)(2,1)S(1)}, bf16[512,1408]{1,0:T(8,128)(2,1)S(1)}, u32[]{:S(2)}, u32[]{:S(2)}) %collective-permute-start.37) | collective-permute-done | bytes 1441824 | tf_op jit(solution)/shard_map/ppermute | solution.py:76
  323.3 28.6 %collective-permute-done.31 = bf16[512,1408]{1,0:T(8,128)(2,1)S(1)} collective-permute-done((bf16[512,1408]{1,0:T(8,128)(2,1)S(1)}, bf16[512,1408]{1,0:T(8,128)(2,1)S(1)}, u32[]{:S(2)}, u32[]{:S(2)}) %collective-permute-start.31) | collective-permute-done | bytes 1441824 | tf_op jit(solution)/shard_map/ppermute | solution.py:76
  356.3 15.2 %collective-permute-done.45 = bf16[1408,256]{1,0:T(8,128)(2,1)S(1)} collective-permute-done((bf16[1408,256]{1,0:T(8,128)(2,1)S(1)}, bf16[1408,256]{1,0:T(8,128)(2,1)S(1)}, u32[]{:S(2)}, u32[]{:S(2)}) %collective-permute-start.45) | collective-permute-done | bytes 720928 | tf_op jit(solution)/shard_map/ppermute | solution.py:81
  373.3 13.7 %collective-permute-done.32 = bf16[256,1408]{1,0:T(8,128)(2,1)S(1)} collective-permute-done((bf16[256,1408]{1,0:T(8,128)(2,1)S(1)}, bf16[256,1408]{1,0:T(8,128)(2,1)S(1)}, u32[]{:S(2)}, u32[]{:S(2)}) %collective-permute-start.32) | collective-permute-done | bytes 720928 | tf_op jit(solution)/shard_map/ppermute | solution.py:76
  388.6 13.8 %collective-permute-done.39 = bf16[256,1408]{1,0:T(8,128)(2,1)S(1)} collective-permute-done((bf16[256,1408]{1,0:T(8,128)(2,1)S(1)}, bf16[256,1408]{1,0:T(8,128)(2,1)S(1)}, u32[]{:S(2)}, u32[]{:S(2)}) %collective-permute-start.39) | collective-permute-done | bytes 720928 | tf_op jit(solution)/shard_map/ppermute | solution.py:81
  404.2 12.4 %collective-permute-done.33 = bf16[256,1408]{1,0:T(8,128)(2,1)S(1)} collective-permute-done((bf16[256,1408]{1,0:T(8,128)(2,1)S(1)}, bf16[256,1408]{1,0:T(8,128)(2,1)S(1)}, u32[]{:S(2)}, u32[]{:S(2)}) %collective-permute-start.33) | collective-permute-done | bytes 720928 | tf_op jit(solution)/shard_map/ppermute | solution.py:81
  419.7 4.8 convolution_convert_fusion.1
  424.5 12.7 %collective-permute-done.40 = bf16[512,1408]{1,0:T(8,128)(2,1)S(1)} collective-permute-done((bf16[512,1408]{1,0:T(8,128)(2,1)S(1)}, bf16[512,1408]{1,0:T(8,128)(2,1)S(1)}, u32[]{:S(2)}, u32[]{:S(2)}) %collective-permute-start.40) | collective-permute-done | bytes 1441824 | tf_op jit(solution)/shard_map/ppermute | solution.py:81
  439.8 25.0 %collective-permute-done.34 = bf16[512,1408]{1,0:T(8,128)(2,1)S(1)} collective-permute-done((bf16[512,1408]{1,0:T(8,128)(2,1)S(1)}, bf16[512,1408]{1,0:T(8,128)(2,1)S(1)}, u32[]{:S(2)}, u32[]{:S(2)}) %collective-permute-start.34) | collective-permute-done | bytes 1441824 | tf_op jit(solution)/shard_map/ppermute | solution.py:81
  469.0 5.9 maximum_convert_fusion.2
  474.9 7.2 reduce_sum.160
  482.1 5.5 fusion.19
  487.6 3.6 convert_add_fusion.4
  495.5 3.6 fusion.28
  499.3 4.9 fusion.25
  506.0 5.1 fusion.12
  511.1 4.5 fusion.46
  515.6 4.6 fusion.48
  520.3 4.6 fusion.58
  524.9 20.9 %multiply_reduce_fusion.2 = (f32[512]{0:T(512)S(1)}, f32[512]{0:T(512)S(1)}, f32[512]{0:T(512)S(1)}, f32[512]{0:T(512)S(1)}, f32[512,4096]{1,0:T(8,128)}) fusion(f32[512,4096]{1,0:T(8,128)} %copy-done.8, f32[512]{0:T(512)S(1)} %copy-done.81, s32[512]{0:T(512)S(1)} %copy-done.78, pred[4096]{0:T(1024)(128)(4,1)S(1)} %bitcast.96, s32[512]{0:T(512)S(1)} %copy-done.76, ...), kind=kOutput, calls=%fused_computation.7 | convolution fusion | flops 578811904 | bytes 68329472 | tf_op jit(solution)/shard_map/dot_general | solution.py:50
  545.9 9.8 %multiply_convert_fusion = bf16[512,4096]{1,0:T(8,128)(2,1)} fusion(f32[512,4096]{1,0:T(8,128)} %fusion.46, f32[512]{0:T(512)S(1)} %get-tuple-element.18, f32[512,4096]{1,0:T(8,128)} %copy-done.10, f32[512]{0:T(512)S(1)} %copy-done.85, s32[512]{0:T(512)S(1)} %copy-done.78, pred[4096]{0:T(1024)(128)(4,1)S(1)} %bitcast.97, s32[512]{0:T(512)S(1)} %copy-done.76, ...), kind=kLoop, calls=%fused_computation | loop fusion | flops 18874368 | bytes 21000192 | tf_op jit(solution)/shard_map/convert_element_type | solution.py:234
  555.7 19.3 %multiply_convert_fusion.2 = (bf16[512,4096]{1,0:T(8,128)(2,1)S(1)}, bf16[512,4096]{1,0:T(8,128)(2,1)}, bf16[512,4096]{1,0:T(8,128)(2,1)}) fusion(f32[512,4096]{1,0:T(8,128)} %get-tuple-element.94, f32[512]{0:T(512)S(1)} %get-tuple-element.15, f32[512,4096]{1,0:T(8,128)} %copy-done.8, f32[512]{0:T(512)S(1)} %copy-done.81, s32[512]{0:T(512)S(1)} %copy-done.78, ...), kind=kLoop, calls=%fused_computation.6 | loop fusion | flops 39845888 | bytes 62951424 | tf_op jit(solution)/shard_map/convert_element_type | solution.py:234
  575.0 3.1 fusion.85
  592.3 4.7 fusion.13
  609.1 5.5 broadcast_select_fusion.3
  614.9 5.1 collective-permute-done.22
  621.7 14.4 %collective-permute-done.4 = bf16[512,512]{1,0:T(8,128)(2,1)S(1)} collective-permute-done((bf16[512,512]{1,0:T(8,128)(2,1)S(1)}, bf16[512,512]{1,0:T(8,128)(2,1)S(1)}, u32[]{:S(2)}, u32[]{:S(2)}) %collective-permute-start.4) | collective-permute-done | bytes 524320 | tf_op jit(solution)/shard_map/ppermute | solution.py:76
  638.6 5.2 maximum_convert_fusion.1
  647.6 5.0 collective-permute-done.24
  652.7 3.6 collective-permute-start.25
  656.3 5.0 collective-permute-done.6
  662.9 5.6 broadcast_select_fusion.5
  670.4 7.5 collective-permute-done.7
  678.3 5.2 maximum_convert_fusion
  704.7 5.5 collective-permute-done.10
  717.2 4.0 collective-permute-done.17
  726.9 5.7 collective-permute-done.13
  740.2 114.4 %all-reduce.6.cloned.1.call-done = (bf16[512,2048]{1,0:T(8,128)(2,1)}, bf16[512,2048]{1,0:T(8,128)(2,1)}) async-done(((bf16[512,2048]{1,0:T(8,128)(2,1)}, bf16[512,2048]{1,0:T(8,128)(2,1)}), (bf16[512,2048]{1,0:T(8,128)(2,1)}, bf16[512,2048]{1,0:T(8,128)(2,1)})) %all-reduce.6.cloned.1.call-update) | async-done | bytes 4194320 | tf_op jit(solution)/shard_map/psum | solution.py:193
  854.6 3.5 fusion.20
  864.8 6.2 fusion.21
  (453 shorter events, 163.7 us)
Async XLA Ops:
  7.2 93.8 %copy-start = (bf16[512,2048]{1,0:T(8,128)(2,1)S(1)}, bf16[512,2048]{1,0:T(8,128)(2,1)}, u32[]{:S(2)}) copy-start(bf16[512,2048]{1,0:T(8,128)(2,1)} %param.20) | copy-start | bytes 6291460
  7.2 52.7 %all-gather.5.cloned.1.call-start = ((), (), s32[]{:S(2)}) async-start(), calls=%async_computation.1 | async-start | bytes 4718592 | tf_op jit(solution)/shard_map/all_gather | solution.py:165
  11.8 68.5 %copy-start.58 = (s32[2,2,8,128]{3,1,2,0:T(2,128)}, s32[2,2,8,128]{3,1,2,0:T(2,128)S(1)}, u32[]{:S(2)}) copy-start(s32[2,2,8,128]{3,1,2,0:T(2,128)S(1)} %copy.24) | copy-start | bytes 49156
  16.4 63.9 %copy-start.75 = (s32[512]{0:T(512)}, s32[512]{0:T(512)S(1)}, u32[]{:S(2)}) copy-start(s32[512]{0:T(512)S(1)} %get-tuple-element.22) | copy-start | bytes 6148
  19.7 170.3 %all-reduce.4.cloned.1.call-start = ((), (), s32[]{:S(2)}) async-start(), calls=%async_computation.2 | async-start | bytes 4194304 | tf_op jit(solution)/shard_map/psum | solution.py:183
  19.7 472.8 %copy-start.69 = (f32[512]{0:T(512)}, f32[512]{0:T(512)S(1)}, u32[]{:S(2)}) copy-start(f32[512]{0:T(512)S(1)} %get-tuple-element.84) | copy-start | bytes 6148
  30.5 49.8 %copy-start.71 = (pred[1,4,8,128]{3,1,2,0:T(4,128)(4,1)}, pred[1,4,8,128]{3,1,2,0:T(4,128)(4,1)S(1)}, u32[]{:S(2)}) copy-start(pred[1,4,8,128]{3,1,2,0:T(4,128)(4,1)S(1)} %copy.25) | copy-start | bytes 12292
  30.5 49.8 %copy-start.77 = (s32[512]{0:T(512)}, s32[512]{0:T(512)S(1)}, u32[]{:S(2)}) copy-start(s32[512]{0:T(512)S(1)} %iota_add_fusion) | copy-start | bytes 6148
  34.5 45.8 %copy-start.42 = (bf16[512,4,128]{0,2,1:T(8,128)(2,1)}, bf16[512,4,128]{0,2,1:T(8,128)(2,1)S(1)}, u32[]{:S(2)}) copy-start(bf16[512,4,128]{0,2,1:T(8,128)(2,1)S(1)} %pad_maximum_fusion.10) | copy-start | bytes 1572868
  103.6 371.2 %all-gather.7.cloned.1.call-start = ((), (), s32[]{:S(2)}) async-start(), calls=%async_computation.4 | async-start | bytes 10485760 | tf_op jit(solution)/shard_map/all_gather | solution.py:13
  220.5 30.2 %collective-permute-start.42 = (bf16[1408,1024]{1,0:T(8,128)(2,1)}, bf16[1408,1024]{1,0:T(8,128)(2,1)}, u32[]{:S(2)}, u32[]{:S(2)}) collective-permute-start(bf16[1408,1024]{1,0:T(8,128)(2,1)} %dynamic-slice_convert_fusion), channel_id=1, source_target_pairs={{0,4},{4,0},{8,12},{12,8},{16,20},{20,16},{24,28},{28,24},{1,5},{5... | collective-permute-start | bytes 8650760 | tf_op jit(solution)/shard_map/ppermute | solution.py:76
  229.2 28.3 %collective-permute-start.36 = (bf16[1024,1408]{1,0:T(8,128)(2,1)}, bf16[1024,1408]{1,0:T(8,128)(2,1)}, u32[]{:S(2)}, u32[]{:S(2)}) collective-permute-start(bf16[1024,1408]{1,0:T(8,128)(2,1)} %dynamic-slice_convert_fusion.1), channel_id=1, source_target_pairs={{0,4},{4,0},{8,12},{12,8},{16,20},{20,16},{24,28},{28,24},{1,5},{5... | collective-permute-start | bytes 8650760 | tf_op jit(solution)/shard_map/ppermute | solution.py:76
  242.1 21.3 %collective-permute-start.30 = (bf16[1024,1408]{1,0:T(8,128)(2,1)}, bf16[1024,1408]{1,0:T(8,128)(2,1)}, u32[]{:S(2)}, u32[]{:S(2)}) collective-permute-start(bf16[1024,1408]{1,0:T(8,128)(2,1)} %dynamic-slice_convert_fusion.2), channel_id=1, source_target_pairs={{0,4},{4,0},{8,12},{12,8},{16,20},{20,16},{24,28},{28,24},{1,5},{5... | collective-permute-start | bytes 8650760 | tf_op jit(solution)/shard_map/ppermute | solution.py:76
  250.7 437.9 %reduce-scatter.2.cloned.1.call-start = ((), (), s32[]{:S(2)}) async-start(), calls=%async_computation.3 | async-start | bytes 4718592 | tf_op jit(solution)/shard_map/reduce_scatter | solution.py:244
  256.0 34.5 %collective-permute-start.43 = (bf16[1408,512]{1,0:T(8,128)(2,1)S(1)}, bf16[1408,512]{1,0:T(8,128)(2,1)S(1)}, u32[]{:S(2)}, u32[]{:S(2)}) collective-permute-start(bf16[1408,512]{1,0:T(8,128)(2,1)S(1)} %dynamic-slice_convert_fusion.3), channel_id=1, source_target_pairs={{0,8},{4,12},{8,0},{12,4},{16,24},{20,28},{24,16},{28,20},{1,9},{5... | collective-permute-start | bytes 4325384 | tf_op jit(solution)/shard_map/ppermute | solution.py:76
  262.6 58.8 %collective-permute-start.37 = (bf16[512,1408]{1,0:T(8,128)(2,1)S(1)}, bf16[512,1408]{1,0:T(8,128)(2,1)S(1)}, u32[]{:S(2)}, u32[]{:S(2)}) collective-permute-start(bf16[512,1408]{1,0:T(8,128)(2,1)S(1)} %dynamic-slice_convert_fusion.4), channel_id=1, source_target_pairs={{0,8},{4,12},{8,0},{12,4},{16,24},{20,28},{24,16},{28,20},{1,9},{5... | collective-permute-start | bytes 4325384 | tf_op jit(solution)/shard_map/ppermute | solution.py:76
  267.6 84.3 %collective-permute-start.31 = (bf16[512,1408]{1,0:T(8,128)(2,1)S(1)}, bf16[512,1408]{1,0:T(8,128)(2,1)S(1)}, u32[]{:S(2)}, u32[]{:S(2)}) collective-permute-start(bf16[512,1408]{1,0:T(8,128)(2,1)S(1)} %dynamic-slice_convert_fusion.5), channel_id=1, source_target_pairs={{0,8},{4,12},{8,0},{12,4},{16,24},{20,28},{24,16},{28,20},{1,9},{5... | collective-permute-start | bytes 4325384 | tf_op jit(solution)/shard_map/ppermute | solution.py:76
  291.1 61.1 %collective-permute-start.44 = (bf16[1408,256]{1,0:T(8,128)(2,1)S(1)}, bf16[1408,256]{1,0:T(8,128)(2,1)S(1)}, u32[]{:S(2)}, u32[]{:S(2)}) collective-permute-start(bf16[1408,256]{1,0:T(8,128)(2,1)S(1)} %dynamic-slice_convert_fusion.8), channel_id=1, source_target_pairs={{0,16},{4,20},{8,24},{12,28},{16,0},{20,4},{24,8},{28,12},{1,17},{... | collective-permute-start | bytes 2162696 | tf_op jit(solution)/shard_map/ppermute | solution.py:76
  321.7 33.0 %collective-permute-start.38 = (bf16[256,1408]{1,0:T(8,128)(2,1)S(1)}, bf16[256,1408]{1,0:T(8,128)(2,1)S(1)}, u32[]{:S(2)}, u32[]{:S(2)}) collective-permute-start(bf16[256,1408]{1,0:T(8,128)(2,1)S(1)} %dynamic-slice_convert_fusion.9), channel_id=1, source_target_pairs={{0,16},{4,20},{8,24},{12,28},{16,0},{20,4},{24,8},{28,12},{1,17},{... | collective-permute-start | bytes 2162696 | tf_op jit(solution)/shard_map/ppermute | solution.py:76
  352.4 19.1 %collective-permute-start.45 = (bf16[1408,256]{1,0:T(8,128)(2,1)S(1)}, bf16[1408,256]{1,0:T(8,128)(2,1)S(1)}, u32[]{:S(2)}, u32[]{:S(2)}) collective-permute-start(bf16[1408,256]{1,0:T(8,128)(2,1)S(1)} %add_convert_fusion.3), channel_id=1, source_target_pairs={{0,16},{4,20},{8,24},{12,28},{16,0},{20,4},{24,8},{28,12},{1,17},{... | collective-permute-start | bytes 2162696 | tf_op jit(solution)/shard_map/ppermute | solution.py:81
  354.0 32.9 %collective-permute-start.32 = (bf16[256,1408]{1,0:T(8,128)(2,1)S(1)}, bf16[256,1408]{1,0:T(8,128)(2,1)S(1)}, u32[]{:S(2)}, u32[]{:S(2)}) collective-permute-start(bf16[256,1408]{1,0:T(8,128)(2,1)S(1)} %dynamic-slice_convert_fusion.10), channel_id=1, source_target_pairs={{0,16},{4,20},{8,24},{12,28},{16,0},{20,4},{24,8},{28,12},{1,17},{... | collective-permute-start | bytes 2162696 | tf_op jit(solution)/shard_map/ppermute | solution.py:76
  354.8 47.6 %collective-permute-start.39 = (bf16[256,1408]{1,0:T(8,128)(2,1)S(1)}, bf16[256,1408]{1,0:T(8,128)(2,1)S(1)}, u32[]{:S(2)}, u32[]{:S(2)}) collective-permute-start(bf16[256,1408]{1,0:T(8,128)(2,1)S(1)} %add_convert_fusion.4), channel_id=1, source_target_pairs={{0,16},{4,20},{8,24},{12,28},{16,0},{20,4},{24,8},{28,12},{1,17},{... | collective-permute-start | bytes 2162696 | tf_op jit(solution)/shard_map/ppermute | solution.py:81
  371.7 45.1 %collective-permute-start.46 = (bf16[1408,512]{1,0:T(8,128)(2,1)S(1)}, bf16[1408,512]{1,0:T(8,128)(2,1)S(1)}, u32[]{:S(2)}, u32[]{:S(2)}) collective-permute-start(bf16[1408,512]{1,0:T(8,128)(2,1)S(1)} %pad_maximum_fusion.6), channel_id=1, source_target_pairs={{0,8},{4,12},{8,0},{12,4},{16,24},{20,28},{24,16},{28,20},{1,9},{5... | collective-permute-start | bytes 4325384 | tf_op jit(solution)/shard_map/ppermute | solution.py:81
  387.1 29.5 %collective-permute-start.33 = (bf16[256,1408]{1,0:T(8,128)(2,1)S(1)}, bf16[256,1408]{1,0:T(8,128)(2,1)S(1)}, u32[]{:S(2)}, u32[]{:S(2)}) collective-permute-start(bf16[256,1408]{1,0:T(8,128)(2,1)S(1)} %add_convert_fusion.5), channel_id=1, source_target_pairs={{0,16},{4,20},{8,24},{12,28},{16,0},{20,4},{24,8},{28,12},{1,17},{... | collective-permute-start | bytes 2162696 | tf_op jit(solution)/shard_map/ppermute | solution.py:81
  402.7 34.5 %collective-permute-start.40 = (bf16[512,1408]{1,0:T(8,128)(2,1)S(1)}, bf16[512,1408]{1,0:T(8,128)(2,1)S(1)}, u32[]{:S(2)}, u32[]{:S(2)}) collective-permute-start(bf16[512,1408]{1,0:T(8,128)(2,1)S(1)} %pad_maximum_fusion.5), channel_id=1, source_target_pairs={{0,8},{4,12},{8,0},{12,4},{16,24},{20,28},{24,16},{28,20},{1,9},{5... | collective-permute-start | bytes 4325384 | tf_op jit(solution)/shard_map/ppermute | solution.py:81
  417.9 49.6 %collective-permute-start.47 = (bf16[1408,1024]{1,0:T(8,128)(2,1)S(1)}, bf16[1408,1024]{1,0:T(8,128)(2,1)S(1)}, u32[]{:S(2)}, u32[]{:S(2)}) collective-permute-start(bf16[1408,1024]{1,0:T(8,128)(2,1)S(1)} %pad_maximum_fusion.3), channel_id=1, source_target_pairs={{0,4},{4,0},{8,12},{12,8},{16,20},{20,16},{24,28},{28,24},{1,5},{5... | collective-permute-start | bytes 8650760 | tf_op jit(solution)/shard_map/ppermute | solution.py:81
  418.1 46.8 %collective-permute-start.34 = (bf16[512,1408]{1,0:T(8,128)(2,1)S(1)}, bf16[512,1408]{1,0:T(8,128)(2,1)S(1)}, u32[]{:S(2)}, u32[]{:S(2)}) collective-permute-start(bf16[512,1408]{1,0:T(8,128)(2,1)S(1)} %pad_maximum_fusion.4), channel_id=1, source_target_pairs={{0,8},{4,12},{8,0},{12,4},{16,24},{20,28},{24,16},{28,20},{1,9},{5... | collective-permute-start | bytes 4325384 | tf_op jit(solution)/shard_map/ppermute | solution.py:81
  437.8 27.7 %copy-start.26 = (bf16[512,1408]{1,0:T(8,128)(2,1)}, bf16[512,1408]{1,0:T(8,128)(2,1)S(1)}, u32[]{:S(2)}) copy-start(bf16[512,1408]{1,0:T(8,128)(2,1)S(1)} %get-tuple-element.35) | copy-start | bytes 4325380
  439.8 169.3 %collective-permute-start.41 = (bf16[1024,1408]{1,0:T(8,128)(2,1)}, bf16[1024,1408]{1,0:T(8,128)(2,1)}, u32[]{:S(2)}, u32[]{:S(2)}) collective-permute-start(bf16[1024,1408]{1,0:T(8,128)(2,1)} %pad_maximum_fusion.2), channel_id=1, source_target_pairs={{0,4},{4,0},{8,12},{12,8},{16,20},{20,16},{24,28},{28,24},{1,5},{5... | collective-permute-start | bytes 8650760 | tf_op jit(solution)/shard_map/ppermute | solution.py:81
  467.5 195.4 %collective-permute-start.35 = (bf16[1024,1408]{1,0:T(8,128)(2,1)}, bf16[1024,1408]{1,0:T(8,128)(2,1)}, u32[]{:S(2)}, u32[]{:S(2)}) collective-permute-start(bf16[1024,1408]{1,0:T(8,128)(2,1)} %pad_maximum_fusion.1), channel_id=1, source_target_pairs={{0,4},{4,0},{8,12},{12,8},{16,20},{20,16},{24,28},{28,24},{1,5},{5... | collective-permute-start | bytes 8650760 | tf_op jit(solution)/shard_map/ppermute | solution.py:81
  492.9 32.0 %copy-start.55 = (bf16[512,512]{1,0:T(8,128)(2,1)}, bf16[512,512]{1,0:T(8,128)(2,1)S(1)}, u32[]{:S(2)}) copy-start(bf16[512,512]{1,0:T(8,128)(2,1)S(1)} %convolution_convert_fusion.2) | copy-start | bytes 1572868
  505.4 97.2 %collective-permute-start.21 = (bf16[512,1024]{1,0:T(8,128)(2,1)}, bf16[512,1024]{1,0:T(8,128)(2,1)}, u32[]{:S(2)}, u32[]{:S(2)}) collective-permute-start(bf16[512,1024]{1,0:T(8,128)(2,1)} %dynamic-slice_convert_fusion.6), channel_id=1, source_target_pairs={{0,4},{4,0},{8,12},{12,8},{16,20},{20,16},{24,28},{28,24},{1,5},{5... | collective-permute-start | bytes 3145736 | tf_op jit(solution)/shard_map/ppermute | solution.py:76
  598.2 8.5 collective-permute-start.3
  602.6 252.0 %all-reduce.6.cloned.1.call-start = ((), (), s32[]{:S(2)}) async-start(), calls=%async_computation.5 | async-start | bytes 8388608 | tf_op jit(solution)/shard_map/psum | solution.py:193
  605.2 14.9 %collective-permute-start.22 = (bf16[512,512]{1,0:T(8,128)(2,1)S(1)}, bf16[512,512]{1,0:T(8,128)(2,1)S(1)}, u32[]{:S(2)}, u32[]{:S(2)}) collective-permute-start(bf16[512,512]{1,0:T(8,128)(2,1)S(1)} %dynamic-slice_convert_fusion.11), channel_id=1, source_target_pairs={{0,8},{4,12},{8,0},{12,4},{16,24},{20,28},{24,16},{28,20},{1,9},{5... | collective-permute-start | bytes 1572872 | tf_op jit(solution)/shard_map/ppermute | solution.py:76
  608.4 27.7 %collective-permute-start.4 = (bf16[512,512]{1,0:T(8,128)(2,1)S(1)}, bf16[512,512]{1,0:T(8,128)(2,1)S(1)}, u32[]{:S(2)}, u32[]{:S(2)}) collective-permute-start(bf16[512,512]{1,0:T(8,128)(2,1)S(1)} %dynamic-slice_convert_fusion.14), channel_id=1, source_target_pairs={{0,8},{4,12},{8,0},{12,4},{16,24},{20,28},{24,16},{28,20},{1,9},{5... | collective-permute-start | bytes 1572872 | tf_op jit(solution)/shard_map/ppermute | solution.py:76
  614.7 29.2 %collective-permute-start.27 = (f32[2048]{0:T(1024)S(1)}, f32[2048]{0:T(1024)S(1)}, u32[]{:S(2)}, u32[]{:S(2)}) collective-permute-start(f32[2048]{0:T(1024)S(1)} %copy-done.79), channel_id=1, source_target_pairs={{0,4},{4,0},{8,12},{12,8},{16,20},{20,16},{24,28},{28,24},{1,5},{5... | collective-permute-start | bytes 24584 | tf_op jit(solution)/shard_map/ppermute | solution.py:95
  620.2 17.4 %collective-permute-start.23 = (bf16[512,256]{1,0:T(8,128)(2,1)S(1)}, bf16[512,256]{1,0:T(8,128)(2,1)S(1)}, u32[]{:S(2)}, u32[]{:S(2)}) collective-permute-start(bf16[512,256]{1,0:T(8,128)(2,1)S(1)} %dynamic-slice_convert_fusion.15), channel_id=1, source_target_pairs={{0,16},{4,20},{8,24},{12,28},{16,0},{20,4},{24,8},{28,12},{1,17},{... | collective-permute-start | bytes 786440 | tf_op jit(solution)/shard_map/ppermute | solution.py:76
  636.4 10.0 %collective-permute-start.5 = (bf16[256,512]{1,0:T(8,128)(2,1)S(1)}, bf16[256,512]{1,0:T(8,128)(2,1)S(1)}, u32[]{:S(2)}, u32[]{:S(2)}) collective-permute-start(bf16[256,512]{1,0:T(8,128)(2,1)S(1)} %dynamic-slice_convert_fusion.18), channel_id=1, source_target_pairs={{0,16},{4,20},{8,24},{12,28},{16,0},{20,4},{24,8},{28,12},{1,17},{... | collective-permute-start | bytes 786440 | tf_op jit(solution)/shard_map/ppermute | solution.py:76
  637.7 14.9 %collective-permute-start.24 = (bf16[512,256]{1,0:T(8,128)(2,1)S(1)}, bf16[512,256]{1,0:T(8,128)(2,1)S(1)}, u32[]{:S(2)}, u32[]{:S(2)}) collective-permute-start(bf16[512,256]{1,0:T(8,128)(2,1)S(1)} %add_convert_fusion.6), channel_id=1, source_target_pairs={{0,16},{4,20},{8,24},{12,28},{16,0},{20,4},{24,8},{28,12},{1,17},{... | collective-permute-start | bytes 786440 | tf_op jit(solution)/shard_map/ppermute | solution.py:81
  643.8 24.7 %collective-permute-start.28 = (f32[2048]{0:T(1024)S(1)}, f32[2048]{0:T(1024)S(1)}, u32[]{:S(2)}, u32[]{:S(2)}) collective-permute-start(f32[2048]{0:T(1024)S(1)} %add.328), channel_id=1, source_target_pairs={{0,8},{4,12},{8,0},{12,4},{16,24},{20,28},{24,16},{28,20},{1,9},{5... | collective-permute-start | bytes 24584 | tf_op jit(solution)/shard_map/ppermute | solution.py:95
  646.5 14.8 %collective-permute-start.6 = (bf16[256,512]{1,0:T(8,128)(2,1)S(1)}, bf16[256,512]{1,0:T(8,128)(2,1)S(1)}, u32[]{:S(2)}, u32[]{:S(2)}) collective-permute-start(bf16[256,512]{1,0:T(8,128)(2,1)S(1)} %add_convert_fusion.7), channel_id=1, source_target_pairs={{0,16},{4,20},{8,24},{12,28},{16,0},{20,4},{24,8},{28,12},{1,17},{... | collective-permute-start | bytes 786440 | tf_op jit(solution)/shard_map/ppermute | solution.py:81
  652.7 17.3 %collective-permute-start.25 = (bf16[512,512]{1,0:T(8,128)(2,1)S(1)}, bf16[512,512]{1,0:T(8,128)(2,1)S(1)}, u32[]{:S(2)}, u32[]{:S(2)}) collective-permute-start(bf16[512,512]{1,0:T(8,128)(2,1)S(1)} %pad_maximum_fusion.17), channel_id=1, source_target_pairs={{0,8},{4,12},{8,0},{12,4},{16,24},{20,28},{24,16},{28,20},{1,9},{5... | collective-permute-start | bytes 1572872 | tf_op jit(solution)/shard_map/ppermute | solution.py:81
  661.3 16.6 %collective-permute-start.7 = (bf16[512,512]{1,0:T(8,128)(2,1)S(1)}, bf16[512,512]{1,0:T(8,128)(2,1)S(1)}, u32[]{:S(2)}, u32[]{:S(2)}) collective-permute-start(bf16[512,512]{1,0:T(8,128)(2,1)S(1)} %pad_maximum_fusion.14), channel_id=1, source_target_pairs={{0,8},{4,12},{8,0},{12,4},{16,24},{20,28},{24,16},{28,20},{1,9},{5... | collective-permute-start | bytes 1572872 | tf_op jit(solution)/shard_map/ppermute | solution.py:81
  668.5 14.9 %collective-permute-start.29 = (f32[2048]{0:T(1024)S(1)}, f32[2048]{0:T(1024)S(1)}, u32[]{:S(2)}, u32[]{:S(2)}) collective-permute-start(f32[2048]{0:T(1024)S(1)} %add.329), channel_id=1, source_target_pairs={{0,16},{4,20},{8,24},{12,28},{16,0},{20,4},{24,8},{28,12},{1,17},{... | collective-permute-start | bytes 24584 | tf_op jit(solution)/shard_map/ppermute | solution.py:95
  670.3 13.7 %collective-permute-start.26 = (bf16[512,1024]{1,0:T(8,128)(2,1)S(1)}, bf16[512,1024]{1,0:T(8,128)(2,1)S(1)}, u32[]{:S(2)}, u32[]{:S(2)}) collective-permute-start(bf16[512,1024]{1,0:T(8,128)(2,1)S(1)} %pad_maximum_fusion.9), channel_id=1, source_target_pairs={{0,4},{4,0},{8,12},{12,8},{16,20},{20,16},{24,28},{28,24},{1,5},{5... | collective-permute-start | bytes 3145736 | tf_op jit(solution)/shard_map/ppermute | solution.py:81
  678.2 6.4 collective-permute-start.8
  692.6 6.9 collective-permute-start.9
  695.5 5.8 collective-permute-start.15
  701.0 9.2 %collective-permute-start.10 = (bf16[512,256]{1,0:T(8,128)(2,1)S(1)}, bf16[512,256]{1,0:T(8,128)(2,1)S(1)}, u32[]{:S(2)}, u32[]{:S(2)}) collective-permute-start(bf16[512,256]{1,0:T(8,128)(2,1)S(1)} %dynamic-slice_convert_fusion.17), channel_id=1, source_target_pairs={{0,8},{4,12},{8,0},{12,4},{16,24},{20,28},{24,16},{28,20},{1,9},{5... | collective-permute-start | bytes 786440 | tf_op jit(solution)/shard_map/ppermute | solution.py:76
  702.9 12.0 %collective-permute-start.16 = (bf16[512,256]{1,0:T(8,128)(2,1)S(1)}, bf16[512,256]{1,0:T(8,128)(2,1)S(1)}, u32[]{:S(2)}, u32[]{:S(2)}) collective-permute-start(bf16[512,256]{1,0:T(8,128)(2,1)S(1)} %dynamic-slice_convert_fusion.16), channel_id=1, source_target_pairs={{0,8},{4,12},{8,0},{12,4},{16,24},{20,28},{24,16},{28,20},{1,9},{5... | collective-permute-start | bytes 786440 | tf_op jit(solution)/shard_map/ppermute | solution.py:76
  710.3 6.3 collective-permute-start.11
  715.0 6.2 collective-permute-start.17
  716.6 7.3 collective-permute-start.12
  721.3 5.0 collective-permute-start.18
  724.0 8.6 collective-permute-start.13
  726.4 9.0 %collective-permute-start.19 = (bf16[512,256]{1,0:T(8,128)(2,1)S(1)}, bf16[512,256]{1,0:T(8,128)(2,1)S(1)}, u32[]{:S(2)}, u32[]{:S(2)}) collective-permute-start(bf16[512,256]{1,0:T(8,128)(2,1)S(1)} %pad_maximum_fusion.21), channel_id=1, source_target_pairs={{0,8},{4,12},{8,0},{12,4},{16,24},{20,28},{24,16},{28,20},{1,9},{5... | collective-permute-start | bytes 786440 | tf_op jit(solution)/shard_map/ppermute | solution.py:81
  732.8 5.5 collective-permute-start.14
  735.6 2.9 collective-permute-start.20
  740.2 120.9 %copy-start.88 = (f32[512]{0:T(512)S(1)}, f32[512]{0:T(512)}, u32[]{:S(2)}) copy-start(f32[512]{0:T(512)} %copy-done.87) | copy-start | bytes 6148
  740.2 124.6 %copy-start.70 = (f32[512]{0:T(512)S(1)}, f32[512]{0:T(512)}, u32[]{:S(2)}) copy-start(f32[512]{0:T(512)} %copy-done.69) | copy-start | bytes 6148
  858.1 1.6 collective-permute-start
  859.6 3.7 collective-permute-start.1
  863.3 7.7 collective-permute-start.2
  (97 other events, 542.9 us)
Sparse Core Ops, SparseCore 0:
  19.8 40.0 all-gather.4
  103.8 86.1 all-reduce.3
  250.8 148.7 all-gather.6
  602.7 59.0 reduce-scatter.1
  699.5 155.0 all-reduce.5
